TPU v7x, 128 devices: a whole 4x4x4 slice. The times are simulated.
128 devices in a mesh: frow: 16 (over y, z), fcol: 8 (over x, core).
Axes of the slice: x: 4, y: 4, z: 4, core: 2. Of those that a mesh axis runs over, the one named last changes fastest.
Arguments:
- front_orig: float32 [16, 1024, 8, 2048], P('frow', None, 'fcol'), may hold values from -0.1 to 45, as said below
- child_tiles: bfloat16 [8192, 128, 128], P(('frow', 'fcol')), may hold values from -0.25 to 0.25
- tile_target: int32 [8192, 2], P(('frow', 'fcol')), may hold values from 0 to 127, as said below
- tile_rows: int32 [8192, 128], P(('frow', 'fcol')), may hold values from 0 to 127, each once within a row
- tile_cols: int32 [8192, 128], P(('frow', 'fcol')), may hold values from 0 to 127, each once within a row
Outputs:
- front_out: float32 [16, 1024, 8, 2048], P('frow', None, 'fcol')
Inputs may be any that keep to these rules, and one draw needn't show every extreme that they name: `front_orig`: Symmetric; the lower triangle of the front after every tile is added defines a positive definite matrix. `tile_target`: rows come 64 to a device in device order. Column 0 is the owner, frow index times 8 plus fcol index; column 1 the local block on that owner, local block row times 16 plus local block column; the block lies on or below the front's block diagonal. At most 2 tiles of one device go to one owner, and one owner receives exactly 2 from every device.
All inputs are finite; a program needn't handle non-finite values.
Results may differ from a plain program's by a relative error of at most 0.0003.
Values may be sent and summed in bfloat16 or wider, within the bound.
No kernel may reach another device: no remote copies, remote signals or barrier semaphores. Data moves between devices by JAX's collectives and lax.ppermute only.
A program may use at most 128 MiB of HBM per device.

v0:
```python
import jax
import jax.numpy as jnp
from jax import lax
from jax.sharding import PartitionSpec as P

PW = 512
NPANEL = 2
CAP = 2


def as_sent(x):
    return jax.tree.map(lambda a: a.astype(jnp.bfloat16) if a.dtype == jnp.float32 else a, x)


def broadcast(block, axis, source):
    block = jnp.where(lax.axis_index(axis) == source, block, jnp.zeros_like(block))
    return lax.psum(block, axis)


def place_tiles(received):
    tile_block, perm_block, target_block = received
    width = tile_block.shape[-1]
    positions = jnp.arange(width, dtype=jnp.int32)
    row_onehot = (perm_block[:, :, 0, None, :] == positions[:, None]).astype(jnp.bfloat16)
    col_onehot = (perm_block[:, :, 1, None, :] == positions[:, None]).astype(jnp.bfloat16)
    moved = jnp.einsum(
        "abxi,abij->abxj", row_onehot, tile_block, preferred_element_type=jnp.float32
    ).astype(jnp.bfloat16)
    placed = jnp.einsum(
        "abxj,abyj->abxy", moved, col_onehot, preferred_element_type=jnp.float32
    ).astype(jnp.bfloat16)
    return (placed, target_block)


def subtract_product(matrix, row_factor, col_factor):
    product = jnp.dot(
        row_factor, col_factor.T, precision=lax.Precision.HIGH, preferred_element_type=jnp.float32
    )
    return matrix - product


def shards(front_orig, child_tiles, tile_target, tile_rows, tile_cols):
    row_devs = lax.axis_size("frow")
    col_devs = lax.axis_size("fcol")
    owners = row_devs * col_devs
    row_here = lax.axis_index("frow")
    col_here = lax.axis_index("fcol")
    width = child_tiles.shape[1]
    held = child_tiles.shape[0]
    slot_count = owners * CAP
    owner_of = tile_target[:, 0]
    block_of = tile_target[:, 1]
    tile_order = jnp.arange(held, dtype=jnp.int32)
    same_owner = owner_of[:, None] == owner_of[None, :]
    earlier = tile_order[None, :] < tile_order[:, None]
    rank_of = jnp.sum(jnp.where(same_owner & earlier, 1, 0), axis=1).astype(jnp.int32)
    slot_of = owner_of * CAP + rank_of
    slot_match = slot_of[None, :] == jnp.arange(slot_count, dtype=jnp.int32)[:, None]
    source_tile = jnp.sum(jnp.where(slot_match, tile_order[None, :], 0), axis=1)
    filled = jnp.any(slot_match, axis=1)
    own_perms = jnp.stack([tile_rows, tile_cols], axis=1)
    placed_here, _ = place_tiles((child_tiles[None], own_perms[None], block_of[None]))
    placed_here = placed_here[0]
    send_tiles = jnp.where(
        filled[:, None, None],
        jnp.take(placed_here, source_tile, axis=0),
        jnp.zeros((), jnp.bfloat16),
    )
    send_blocks = jnp.where(filled, jnp.take(block_of, source_tile, axis=0), -1)
    placed = lax.all_to_all(
        send_tiles.reshape(owners, CAP, width, width),
        ("frow", "fcol"),
        split_axis=0,
        concat_axis=0,
        tiled=True,
    )
    blocks_in = lax.all_to_all(
        send_blocks.reshape(owners, CAP), ("frow", "fcol"), split_axis=0, concat_axis=0, tiled=True
    )
    local = front_orig[0, :, 0, :]
    row_blocks = local.shape[0] // width
    col_blocks = local.shape[1] // width
    block_ids = jnp.arange(row_blocks * col_blocks, dtype=jnp.int32)
    block_onehot = (blocks_in.reshape(1, slot_count) == block_ids[:, None]).astype(jnp.bfloat16)
    summed = jnp.dot(
        block_onehot, placed.reshape(slot_count, width * width), preferred_element_type=jnp.float32
    )
    added = (
        summed.reshape(row_blocks, col_blocks, width, width)
        .transpose(0, 2, 1, 3)
        .reshape(local.shape)
    )
    matrix = local + added
    first_ids = jnp.arange(row_blocks, dtype=jnp.int32) * col_blocks
    first_onehot = (blocks_in.reshape(1, slot_count) == first_ids[:, None]).astype(jnp.bfloat16)
    first_added = jnp.dot(
        first_onehot, placed.reshape(slot_count, width * width), preferred_element_type=jnp.float32
    ).reshape(local.shape[0], width)
    first_column = local[:, :width] + first_added
    local_rows = jnp.arange(local.shape[0], dtype=jnp.int32)
    local_cols = jnp.arange(local.shape[1], dtype=jnp.int32)
    global_rows = (local_rows // width * row_devs + row_here) * width + local_rows % width
    global_cols = (local_cols // width * col_devs + col_here) * width + local_cols % width
    total = NPANEL * PW
    hi = lax.Precision.HIGH
    first_row = lax.all_gather(
        first_column[:width].astype(jnp.bfloat16), "fcol", axis=1, tiled=True
    )[:, :total]
    split = total // 2
    left = lax.all_gather(first_row[:, :split], "frow", axis=0, tiled=True)[:total]
    left, right_src, matrix = lax.optimization_barrier((left, first_row[:, split:], matrix))
    right = lax.all_gather(right_src, "frow", axis=0, tiled=True)[:total]
    right, own_column = lax.optimization_barrier((right, first_column))
    halves = [left.astype(jnp.float32), right.astype(jnp.float32)]
    row_panel = lax.all_gather(own_column.astype(jnp.bfloat16), "fcol", axis=1, tiled=True)[
        :, :total
    ]
    half = row_devs // col_devs
    pairs = []
    for src_row in range(row_devs):
        for src_col in range(col_devs):
            dst_row = src_row // col_devs * col_devs + src_col
            dst_col = src_row % col_devs
            pairs.append((src_row * col_devs + src_col, dst_row * col_devs + dst_col))
    piece = lax.dynamic_slice_in_dim(row_panel, col_here * width, width, axis=0)
    piece = lax.ppermute(piece, ("frow", "fcol"), pairs)
    col_all = lax.all_gather(piece, "frow", axis=0, tiled=False)
    col_panel = (
        col_all.reshape(half, row_blocks, width, total)
        .transpose(1, 0, 2, 3)
        .reshape(local.shape[1], total)
    )
    rows_all = jnp.concatenate([row_panel, col_panel], axis=0).astype(jnp.float32)
    n_own = local.shape[0]
    full = lax.Precision.HIGHEST
    corner_blocks = total // width
    factor_full = jnp.zeros((total, total), jnp.float32)
    eye = jnp.eye(width, dtype=jnp.float32)
    inverses = []
    for h, cur in enumerate(halves):
        if h > 0:
            done_cols = factor_full[:, : h * split]
            cur = cur - jnp.dot(
                done_cols,
                done_cols[h * split : (h + 1) * split].T,
                precision=full,
                preferred_element_type=jnp.float32,
            )
        for b in range(split // width):
            start = h * split + b * width
            stop = start + width
            lb = b * width
            diag_block = cur[start:stop, lb : lb + width]
            symmetric = jnp.tril(diag_block) + jnp.tril(diag_block, -1).T
            factor = jnp.linalg.cholesky(symmetric)
            inverse = lax.linalg.triangular_solve(factor, eye, left_side=True, lower=True)
            inverses.append(inverse)
            factor_full = factor_full.at[start:stop, start:stop].set(factor)
            if stop < total:
                below = jnp.dot(
                    cur[stop:, lb : lb + width],
                    inverse.T,
                    precision=full,
                    preferred_element_type=jnp.float32,
                )
                factor_full = factor_full.at[stop:, start:stop].set(below)
                if lb + width < split:
                    cur = cur.at[stop:, lb + width :].add(
                        -jnp.dot(
                            below,
                            below[: split - lb - width].T,
                            precision=full,
                            preferred_element_type=jnp.float32,
                        )
                    )
    inv_blocks = jnp.stack(inverses)
    size = width
    while size < total:
        pairs_n = total // (2 * size)
        lower_left = jnp.stack(
            [
                factor_full[
                    (2 * k + 1) * size : (2 * k + 2) * size, 2 * k * size : (2 * k + 1) * size
                ]
                for k in range(pairs_n)
            ]
        )
        upper_inv = inv_blocks[0::2]
        lower_inv = inv_blocks[1::2]
        mixed = -jnp.einsum(
            "nab,nbc->nac",
            lower_inv,
            jnp.einsum("nab,nbc->nac", lower_left, upper_inv, precision=full),
            precision=full,
        )
        zeros = jnp.zeros_like(mixed)
        top = jnp.concatenate([upper_inv, zeros], axis=2)
        bottom = jnp.concatenate([mixed, lower_inv], axis=2)
        inv_blocks = jnp.concatenate([top, bottom], axis=1)
        size *= 2
    factor_inverse = inv_blocks[0]
    solved = jnp.dot(rows_all, factor_inverse.T, precision=hi, preferred_element_type=jnp.float32)
    row_factor = solved[:n_own]
    col_factor = solved[n_own:]
    matrix = subtract_product(matrix, row_factor, col_factor)
    corner_rows = lax.dynamic_slice_in_dim(
        factor_full, jnp.minimum(row_here, total // width - 1) * width, width, axis=0
    )
    head = jnp.where(row_here * width < total, corner_rows, row_factor[:width])
    panel_vals = jnp.concatenate([head, row_factor[width:]], axis=0)
    own_part = lax.dynamic_slice_in_dim(panel_vals, col_here * width, width, axis=1)
    matrix = matrix.at[:, :width].set(own_part)
    lower_part = global_rows[:, None] >= global_cols[None, :]
    result = jnp.where(lower_part, matrix, 0.0)
    return result[None, :, None, :]


def solution(mesh):
    return jax.shard_map(
        shards,
        mesh=mesh,
        in_specs=(
            P("frow", None, "fcol", None),
            P(("frow", "fcol"), None, None),
            P(("frow", "fcol"), None),
            P(("frow", "fcol"), None),
            P(("frow", "fcol"), None),
        ),
        out_specs=P("frow", None, "fcol", None),
        check_vma=False,
    )
```

profile of v0, /device:TPU:23, one launch (start us, length us, event | category | flops | bytes accessed | tf_op | source)
XLA Modules:
  0.0 611.7 jit_solution(1710537951863947196)
XLA Ops:
  11.4 10.6 %all-to-all-start = ((s32[128,1,2]{2,1,0:T(1,128)}), s32[128,1,2]{2,1,0:T(1,128)S(1)}, u32[]{:S(2)}, u32[]{:S(2)}) async-start(s32[128,1,2]{2,1,0:T(1,128)} %bitcast.5), calls=%async_computation | async-start | bytes 131072 | tf_op jit(solution)/shard_map/all_to_all | solution.py:77
  23.1 3.6 fusion.28
  26.8 10.2 %gather_fusion.1 = bf16[256,128,128]{2,1,0:T(8,128)(2,1)} fusion(bf16[64,128,128]{2,1,0:T(8,128)(2,1)} %fusion.28, s32[1024]{0:T(1024)S(1)} %pad_clamp_fusion), kind=kCustom, calls=%fused_computation.1 | custom fusion | bytes 16778240 | tf_op jit(solution)/shard_map/jit(_take)/gather | solution.py:66
  37.0 7.4 %select_select_fusion = bf16[128,2,128,128]{3,2,1,0:T(8,128)(2,1)} fusion(bf16[128,2,128,128]{3,2,1,0:T(8,128)(2,1)} %bitcast.217, pred[128,2]{1,0:T(8,128)(4,1)S(1)} %compare_and_fusion, pred[128,2]{1,0:T(8,128)(4,1)S(1)} %broadcast_in_dim.106), kind=kLoop, calls=%fused_computation.7 | loop fusion | flops 8388608 | bytes 16777728 | tf_op jit(solution)/shard_map/jit(_where)/select_n | solution.py:64
  44.4 10.2 %all-to-all-start.1 = ((bf16[128,2,128,128]{3,2,1,0:T(8,128)(2,1)}), bf16[128,2,128,128]{3,2,1,0:T(8,128)(2,1)}, u32[]{:S(2)}, u32[]{:S(2)}) async-start(bf16[128,2,128,128]{3,2,1,0:T(8,128)(2,1)} %select_select_fusion), calls=%async_computation.1 | async-start | bytes 16777216 | tf_op jit(solution)/shard_map/all_to_all | solution.py:70
  55.0 20.7 %copy.246 = f32[1,1024,1,2048]{1,3,2,0:T(8,128)} copy(f32[1,1024,1,2048]{3,2,1,0:T(1,128)} %param.52) | data formatting | bytes 16777216 | tf_op args[0]
  77.0 76.1 %all-to-all-done.1 = bf16[128,2,128,128]{3,2,1,0:T(8,128)(2,1)} async-done(((bf16[128,2,128,128]{3,2,1,0:T(8,128)(2,1)}), bf16[128,2,128,128]{3,2,1,0:T(8,128)(2,1)}, u32[]{:S(2)}, u32[]{:S(2)}) %all-to-all-start.1) | async-done | bytes 8388640 | tf_op jit(solution)/shard_map/all_to_all | solution.py:70
  153.1 7.8 %fusion.143 = f32[8,16384]{1,0:T(8,128)S(1)} fusion(s32[256]{0:T(256)S(1)} %eq.128, s32[8]{0:T(128)S(1)} %iota_multiply_fusion, bf16[32,8,128,128]{3,2,1,0:T(8,128)(2,1)} %bitcast.76), kind=kOutput, calls=%fused_computation.238 | convolution fusion | flops 67110912 | bytes 8913952 | tf_op jit(solution)/shard_map/dot_general | solution.py:96
  162.4 18.7 %all_gather.18 = bf16[128,1024]{0,1:T(8,128)(2,1)S(1)} all-gather(bf16[128,128]{0,1:T(8,128)(2,1)S(1)} %slice.839), channel_id=1, replica_groups=mesh['frow'=16,'fcol'=8] {'fcol'}, dimensions={1}, use_global_device_ids=true | all-gather | bytes 294912 | tf_op jit(solution)/shard_map/all_gather | solution.py:106
  184.6 23.3 %copy.365 = bf16[32,8,128,128]{3,1,2,0:T(8,128)(2,1)} copy(bf16[32,8,128,128]{3,2,1,0:T(8,128)(2,1)} %bitcast.76) | data formatting | bytes 16777216
  207.9 11.9 %copy.249 = bf16[256,16384]{0,1:T(8,128)(2,1)} copy(bf16[256,16384]{1,0:T(8,128)(2,1)} %bitcast.218) | data formatting | bytes 16777216 | tf_op jit(solution)/shard_map/reshape | solution.py:97
  219.8 6.3 %fusion.90 = f32[8,16,128,128]{3,1,2,0:T(8,128)S(1)} fusion(bf16[128,128,256,1]{2,1,0,3:T(8,128)(2,1)} %bitcast.221, s32[8,16]{1,0:T(8,128)S(1)} %multiply_add_fusion, s32[256]{0:T(256)S(1)} %eq.128), kind=kOutput, calls=%fused_computation.113 | convolution fusion | flops 1073774592 | bytes 16778752 | tf_op jit(solution)/shard_map/dot_general | solution.py:85
  226.1 7.5 %copy.364 = f32[128,8,16,128]{3,1,2,0:T(8,128)} copy(f32[128,8,16,128]{3,2,1,0:T(8,128)S(1)} %bitcast.222) | data formatting | bytes 16777216
  233.6 9.3 %copy.343 = f32[1024,2048]{0,1:T(8,128)} copy(f32[1024,2048]{1,0:T(8,128)} %bitcast.219) | data formatting | bytes 16777216 | tf_op jit(solution)/shard_map/reshape | solution.py:91
  242.9 12.1 %bitcast_add_fusion.16 = f32[1024,2048]{0,1:T(8,128)} fusion(f32[1024,2048]{0,1:T(8,128)} %copy.343, f32[1,1024,1,2048]{1,3,2,0:T(8,128)} %copy.246), kind=kLoop, calls=%fused_computation.280 | loop fusion | flops 2097152 | bytes 25165824 | tf_op jit(solution)/shard_map/add | solution.py:93
  257.4 11.7 %cholesky.134 = f32[128,128]{1,0:T(8,128)S(1)} custom-call(f32[128,128]{1,0:T(8,128)S(1)} %copy.258), custom_call_target="Cholesky" | custom-call | tf_op jit(solution)/shard_map/jit(cholesky)/cholesky | solution.py:155
  270.9 9.8 %custom-call.12 = f32[1,128,128]{1,2,0:T(8,128)S(1)} custom-call(f32[1,128,128]{2,1,0:T(8,128)S(1)} %copy.261), custom_call_target="InvertDiagBlocksLowerTriangular" | custom-call | tf_op jit(solution)/shard_map/triangular_solve/custom-call.0 | solution.py:156
  282.8 2.0 copy.289
  284.8 2.3 fusion.34
  288.2 11.9 %cholesky.145 = f32[128,128]{1,0:T(8,128)S(1)} custom-call(f32[128,128]{1,0:T(8,128)S(1)} %copy.268), custom_call_target="Cholesky" | custom-call | tf_op jit(solution)/shard_map/jit(cholesky)/cholesky | solution.py:155
  300.2 2.5 scatter.54
  305.8 9.8 %custom-call.13 = f32[1,128,128]{1,2,0:T(8,128)S(1)} custom-call(f32[1,128,128]{2,1,0:T(8,128)S(1)} %copy.271), custom_call_target="InvertDiagBlocksLowerTriangular" | custom-call | tf_op jit(solution)/shard_map/triangular_solve/custom-call.0 | solution.py:156
  318.6 11.7 %cholesky.156 = f32[128,128]{1,0:T(8,128)S(1)} custom-call(f32[128,128]{1,0:T(8,128)S(1)} %copy.278), custom_call_target="Cholesky" | custom-call | tf_op jit(solution)/shard_map/jit(cholesky)/cholesky | solution.py:155
  333.5 9.8 %custom-call.14 = f32[1,128,128]{1,2,0:T(8,128)S(1)} custom-call(f32[1,128,128]{2,1,0:T(8,128)S(1)} %copy.281), custom_call_target="InvertDiagBlocksLowerTriangular" | custom-call | tf_op jit(solution)/shard_map/triangular_solve/custom-call.0 | solution.py:156
  346.2 11.7 %cholesky.167 = f32[128,128]{1,0:T(8,128)S(1)} custom-call(f32[128,128]{1,0:T(8,128)S(1)} %fusion.105), custom_call_target="Cholesky" | custom-call | tf_op jit(solution)/shard_map/jit(cholesky)/cholesky | solution.py:155
  361.0 9.8 %custom-call.15 = f32[1,128,128]{1,2,0:T(8,128)S(1)} custom-call(f32[1,128,128]{2,1,0:T(8,128)S(1)} %copy.288), custom_call_target="InvertDiagBlocksLowerTriangular" | custom-call | tf_op jit(solution)/shard_map/triangular_solve/custom-call.0 | solution.py:156
  373.7 5.4 fusion.31
  381.7 11.7 %cholesky.178 = f32[128,128]{1,0:T(8,128)S(1)} custom-call(f32[128,128]{1,0:T(8,128)S(1)} %fusion.103), custom_call_target="Cholesky" | custom-call | tf_op jit(solution)/shard_map/jit(cholesky)/cholesky | solution.py:155
  395.6 9.8 %custom-call.16 = f32[1,128,128]{1,2,0:T(8,128)S(1)} custom-call(f32[1,128,128]{2,1,0:T(8,128)S(1)} %copy.299), custom_call_target="InvertDiagBlocksLowerTriangular" | custom-call | tf_op jit(solution)/shard_map/triangular_solve/custom-call.0 | solution.py:156
  408.1 2.1 collective-permute-start
  412.1 16.0 %collective-permute-done = bf16[128,1024]{0,1:T(8,128)(2,1)S(1)} collective-permute-done((bf16[128,1024]{0,1:T(8,128)(2,1)S(1)}, bf16[128,1024]{0,1:T(8,128)(2,1)S(1)}, u32[]{:S(2)}, u32[]{:S(2)}) %collective-permute-start) | collective-permute-done | bytes 262176 | tf_op jit(solution)/shard_map/ppermute | solution.py:126
  429.0 11.7 %cholesky.189 = f32[128,128]{1,0:T(8,128)S(1)} custom-call(f32[128,128]{1,0:T(8,128)S(1)} %fusion.101), custom_call_target="Cholesky" | custom-call | tf_op jit(solution)/shard_map/jit(cholesky)/cholesky | solution.py:155
  443.7 9.8 %custom-call.17 = f32[1,128,128]{1,2,0:T(8,128)S(1)} custom-call(f32[1,128,128]{2,1,0:T(8,128)S(1)} %copy.305), custom_call_target="InvertDiagBlocksLowerTriangular" | custom-call | tf_op jit(solution)/shard_map/triangular_solve/custom-call.0 | solution.py:156
  454.9 11.7 %cholesky.200 = f32[128,128]{1,0:T(8,128)S(1)} custom-call(f32[128,128]{1,0:T(8,128)S(1)} %fusion.99), custom_call_target="Cholesky" | custom-call | tf_op jit(solution)/shard_map/jit(cholesky)/cholesky | solution.py:155
  469.5 10.0 %custom-call.18 = f32[1,128,128]{1,2,0:T(8,128)S(1)} custom-call(f32[1,128,128]{2,1,0:T(8,128)S(1)} %copy.311), custom_call_target="InvertDiagBlocksLowerTriangular" | custom-call | tf_op jit(solution)/shard_map/triangular_solve/custom-call.0 | solution.py:156
  480.8 11.7 %cholesky.211 = f32[128,128]{1,0:T(8,128)S(1)} custom-call(f32[128,128]{1,0:T(8,128)S(1)} %fusion.97), custom_call_target="Cholesky" | custom-call | tf_op jit(solution)/shard_map/jit(cholesky)/cholesky | solution.py:155
  493.8 9.8 %custom-call.19 = f32[1,128,128]{1,2,0:T(8,128)S(1)} custom-call(f32[1,128,128]{2,1,0:T(8,128)S(1)} %get-tuple-element.281), custom_call_target="InvertDiagBlocksLowerTriangular" | custom-call | tf_op jit(solution)/shard_map/triangular_solve/custom-call.0 | solution.py:156
  510.9 3.5 fusion.42
  517.8 2.9 copy.252
  520.7 5.6 copy.360
  526.2 6.7 %copy.251 = bf16[2,8,128,1024]{3,2,0,1:T(8,128)(2,1)} copy(bf16[2,8,128,1024]{2,1,0,3:T(8,128)(2,1)} %bitcast.220) | data formatting | bytes 8388608 | tf_op jit(solution)/shard_map/reshape | solution.py:129
  532.9 16.6 %fusion.2 = f32[3072,1024]{1,0:T(8,128)S(1)} fusion(bf16[2048,1024]{1,0:T(8,128)(2,1)} %bitcast.224, bf16[1024,1024]{1,0:T(8,128)(2,1)S(1)} %copy.252, f32[1,512,512]{2,1,0:T(8,128)} %get-tuple-element.292, f32[1,512,512]{2,1,0:T(8,128)} %get-tuple-element.291, f32[1,512,512]{2,1,0:T(8,128)S(1)} %fusion.35), kind=kOutput, calls=%fused_computation.8 | convolution fusion | flops 19344130048 | bytes 22020096 | tf_op jit(solution)/shard_map/dot_general | solution.py:202
  549.6 2.3 slice.757
  551.9 17.7 %fusion.15 = f32[1024,2048]{0,1:T(8,128)} fusion(f32[1024,2048]{0,1:T(8,128)} %bitcast_add_fusion.16, f32[3072,1024]{1,0:T(8,128)S(1)} %fusion.2), kind=kOutput, calls=%fused_computation.26 | convolution fusion | flops 12886999040 | bytes 29360128 | tf_op jit(solution)/shard_map/dot_general | solution.py:36
  569.8 5.0 copy.345
  575.9 2.6 fusion.49
  578.5 5.9 select_bitcast_fusion
  584.5 20.5 %copy.329 = f32[1,1024,1,2048]{3,2,1,0:T(1,128)} copy(f32[1,1024,1,2048]{1,3,2,0:T(8,128)} %select_bitcast_fusion) | data formatting | bytes 16777216 | tf_op jit(solution)/shard_map/broadcast_in_dim | solution.py:215
  (208 shorter events, 69.3 us)
Async XLA Ops:
  6.5 16.6 %copy-start = (bf16[64,128,128]{2,1,0:T(8,128)(2,1)S(1)}, bf16[64,128,128]{2,1,0:T(8,128)(2,1)}, u32[]{:S(2)}) copy-start(bf16[64,128,128]{2,1,0:T(8,128)(2,1)} %param.53) | copy-start | bytes 6291460
  11.4 33.0 %all-to-all-start = ((s32[128,1,2]{2,1,0:T(1,128)}), s32[128,1,2]{2,1,0:T(1,128)S(1)}, u32[]{:S(2)}, u32[]{:S(2)}) async-start(s32[128,1,2]{2,1,0:T(1,128)} %bitcast.5), calls=%async_computation | async-start | bytes 131072 | tf_op jit(solution)/shard_map/all_to_all | solution.py:77
  44.4 108.7 %all-to-all-start.1 = ((bf16[128,2,128,128]{3,2,1,0:T(8,128)(2,1)}), bf16[128,2,128,128]{3,2,1,0:T(8,128)(2,1)}, u32[]{:S(2)}, u32[]{:S(2)}) async-start(bf16[128,2,128,128]{3,2,1,0:T(8,128)(2,1)} %select_select_fusion), calls=%async_computation.1 | async-start | bytes 16777216 | tf_op jit(solution)/shard_map/all_to_all | solution.py:70
  54.6 200.4 %all-gather.6.cloned.1.call-start = ((), (), s32[]{:S(2)}) async-start(), calls=%async_computation.2 | async-start | bytes 2228224 | tf_op jit(solution)/shard_map/all_gather | solution.py:110
  162.3 45.6 %copy-start.5 = (bf16[1024,128]{0,1:T(8,128)(2,1)}, bf16[1024,128]{0,1:T(8,128)(2,1)S(1)}, u32[]{:S(2)}) copy-start(bf16[1024,128]{0,1:T(8,128)(2,1)S(1)} %slice_add_fusion) | copy-start | bytes 786436
  181.8 162.5 %all-gather.8.cloned.1.call-start = ((), (), s32[]{:S(2)}) async-start(), calls=%async_computation.3 | async-start | bytes 2228224 | tf_op jit(solution)/shard_map/all_gather | solution.py:112
  181.9 26.0 %copy-start.10 = (s32[128]{0:T(128)}, s32[128]{0:T(128)S(1)}, u32[]{:S(2)}) copy-start(s32[128]{0:T(128)S(1)} %iota_add_fusion) | copy-start | bytes 1540
  182.1 75.1 %copy-start.6 = (pred[128,128]{0,1:T(8,128)(4,1)}, pred[128,128]{0,1:T(8,128)(4,1)S(1)}, u32[]{:S(2)}) copy-start(pred[128,128]{0,1:T(8,128)(4,1)S(1)} %copy.255) | copy-start | bytes 49156
  256.6 150.5 %all-gather.10.cloned.1.call-start = ((), (), s32[]{:S(2)}) async-start(), calls=%async_computation.4 | async-start | bytes 2359296 | tf_op jit(solution)/shard_map/all_gather | solution.py:115
  287.1 16.4 %copy-start.4 = (f32[896,128]{0,1:T(8,128)S(1)}, f32[896,128]{0,1:T(8,128)}, u32[]{:S(2)}) copy-start(f32[896,128]{0,1:T(8,128)} %copy.289) | copy-start | bytes 1376260
  300.2 18.2 %copy-start.7 = (pred[128,128]{0,1:T(8,128)(4,1)S(1)}, pred[128,128]{0,1:T(8,128)(4,1)}, u32[]{:S(2)}) copy-start(pred[128,128]{0,1:T(8,128)(4,1)} %copy-done.6) | copy-start | bytes 49156
  318.3 27.7 %copy-start.11 = (s32[128]{0:T(128)S(1)}, s32[128]{0:T(128)}, u32[]{:S(2)}) copy-start(s32[128]{0:T(128)} %copy-done.10) | copy-start | bytes 1540
  344.3 28.5 %slice-start = ((bf16[2048,512]{0,1:T(8,128)(2,1)}), bf16[1024,512]{0,1:T(8,128)(2,1)S(1)}, s32[]{:S(2)}) async-start(bf16[2048,512]{0,1:T(8,128)(2,1)} %all-gather.8.cloned.1.call-done), calls=%async_computation.6 | async-start | bytes 2097152 | tf_op jit(solution)/shard_map/slice | solution.py:112
  344.3 176.3 %all-gather.12.cloned.1.call-start = ((), (), s32[]{:S(2)}) async-start(), calls=%async_computation.5 | async-start | bytes 4456448 | tf_op jit(solution)/shard_map/all_gather | solution.py:127
  373.7 31.7 %copy-start.3 = (f32[8,128,128]{2,1,0:T(8,128)S(1)}, f32[8,128,128]{2,1,0:T(8,128)}, u32[]{:S(2)}) copy-start(f32[8,128,128]{2,1,0:T(8,128)} %get-tuple-element.321) | copy-start | bytes 1572868
  379.2 1.4 copy-start.2
  408.1 19.9 %collective-permute-start = (bf16[128,1024]{0,1:T(8,128)(2,1)S(1)}, bf16[128,1024]{0,1:T(8,128)(2,1)S(1)}, u32[]{:S(2)}, u32[]{:S(2)}) collective-permute-start(bf16[128,1024]{0,1:T(8,128)(2,1)S(1)} %constant_dynamic-slice_fusion), channel_id=1, source_target_pairs={{0,0},{1,8},{2,16},{3,24},{4,32},{5,40},{6,48},{7,56},{8,1},{9,9},... | collective-permute-start | bytes 786440 | tf_op jit(solution)/shard_map/ppermute | solution.py:126
  428.0 0.7 copy-start.8
  574.8 3.7 copy-start.9
  574.8 3.7 copy-start.12
  578.5 26.4 %copy-start.1 = (bf16[64,128,128]{2,1,0:T(8,128)(2,1)S(1)}, bf16[64,128,128]{2,1,0:T(8,128)(2,1)}, u32[]{:S(2)}) copy-start(bf16[64,128,128]{2,1,0:T(8,128)(2,1)} %param.53) | copy-start | bytes 6291460
Sparse Core Ops, SparseCore 0:
  181.9 45.7 all-gather.5
  256.8 45.8 all-gather.7
  344.4 24.9 all-gather.9
  428.9 53.5 all-gather.11
where the time goes:
time: 620 us; the launch traced here: 612 us
  other arithmetic  227 us (37%)
  local copies, waits for them, and re-layouts  154 us (25%)
  waiting for transfers between devices  92.2 us (15%)
  matrix products  82.1 us (13%)
  starting transfers between devices  24 us (4%)
  blocking collectives  18.7 us (3%)
  between operations  14.5 us (2%)
    another operation x24, other arithmetic, shards(): factor = jnp.linalg.cholesky(symmetric)  100 us
    another operation x11, other arithmetic, shards(): lax.linalg.triangular_solve(factor, eye, left_side=True, lower=True)  80 us
    all_to_all x1, waiting for transfers between devices, shards(): lax.all_to_all(send_tiles.reshape(owners, CAP, width, width), ('frow', 'f...  76.1 us
    unnamed x32, local copies, waits for them, and re-layouts  64.4 us
    broadcast_in_dim x1, local copies, waits for them, and re-layouts, shards(): return result[None, :, None, :]  20.5 us
    all_gather x1, blocking collectives, shards(): lax.all_gather(first_column[:width].astype(jnp.bfloat16), 'fcol', axis=1,...  18.7 us
    dot_general x1, matrix products, subtract_product(): jnp.dot(row_factor, col_factor.T, precision=lax.Precision.HIGH, preferred...  17.7 us
    dot_general x1, matrix products, shards(): jnp.dot(rows_all, factor_inverse.T, precision=hi, preferred_element_type=...  16.6 us
  transfers between devices with their start and end apart: 7, of which 2 were waited for; matrix products, arithmetic and copies ran while one was open for 59% of the time, Pallas kernels for 0%

commit v1 on v0

--- a/solution.py
+++ b/solution.py
@@ -103,8 +103,14 @@
     global_cols = (local_cols // width * col_devs + col_here) * width + local_cols % width
     total = NPANEL * PW
     hi = lax.Precision.HIGH
-    first_row = lax.all_gather(
-        first_column[:width].astype(jnp.bfloat16), "fcol", axis=1, tiled=True
+    first_row = jnp.concatenate(
+        lax.all_to_all(
+            jnp.stack([first_column[:width].astype(jnp.bfloat16)] * lax.axis_size("fcol")),
+            "fcol",
+            0,
+            0,
+        ),
+        axis=1,
     )[:, :total]
     split = total // 2
     left = lax.all_gather(first_row[:, :split], "frow", axis=0, tiled=True)[:total]

time: 620 us -> 557 us (0.90)
  local copies, waits for them, and re-layouts: 154 us -> 95.4 us
    unnamed x32 -> x22, local copies, waits for them, and re-layouts: 64.4 us -> 41.5 us
    all_gather x1 -> x0, blocking collectives: 18.7 us -> none  [shards(): lax.all_gather(first_column[:width].astype(jnp.bfloat16), 'fcol', axis=1,...]
    all_to_all x0 -> x1, blocking collectives: none -> 14.8 us  [shards(): lax.all_to_all(jnp.stack([first_column[:width].astype(jnp.bfloat16)] * la...]
    ppermute x1, waiting for transfers between devices: 16 us -> 3.89 us  [shards(): piece = lax.ppermute(piece, ('frow', 'fcol'), pairs)]
    all_to_all x1, waiting for transfers between devices: 76.1 us -> 85.8 us  [shards(): lax.all_to_all(send_tiles.reshape(owners, CAP, width, width), ('frow', 'f...]
    reshape x1 -> x0, local copies, waits for them, and re-layouts: 9.27 us -> none  [shards(): added = summed.reshape(row_blocks, col_blocks, width, width).transpose(0,...]
    broadcast_in_dim x1, local copies, waits for them, and re-layouts: 20.5 us -> 12.5 us  [shards(): return result[None, :, None, :]]
    another operation x11 -> x9, other arithmetic: 80 us -> 79.3 us  [shards(): lax.linalg.triangular_solve(factor, eye, left_side=True, lower=True)]
  transfers between devices with their start and end apart: 7 -> 7, of which waited for: 2 -> 2; matrix products, arithmetic and copies ran while one was open for 59% -> 60% of each run, Pallas kernels for 0% -> 0%
where the time goes in v1:
time: 557 us; the launch traced here: 549 us
  other arithmetic  223 us (40%)
  local copies, waits for them, and re-layouts  95.4 us (17%)
  waiting for transfers between devices  89.8 us (16%)
  matrix products  85.8 us (15%)
  starting transfers between devices  26.3 us (5%)
  blocking collectives  14.8 us (3%)
  between operations  14.3 us (3%)
    another operation x24, other arithmetic, shards(): factor = jnp.linalg.cholesky(symmetric)  99.9 us
    all_to_all x1, waiting for transfers between devices, shards(): lax.all_to_all(send_tiles.reshape(owners, CAP, width, width), ('frow', 'f...  85.8 us
    another operation x9, other arithmetic, shards(): lax.linalg.triangular_solve(factor, eye, left_side=True, lower=True)  79.3 us
    unnamed x22, local copies, waits for them, and re-layouts  41.5 us
    dot_general x1, matrix products, subtract_product(): jnp.dot(row_factor, col_factor.T, precision=lax.Precision.HIGH, preferred...  18 us
    add x1, other arithmetic, shards(): matrix = local + added  17.4 us
    all_to_all x1, blocking collectives, shards(): lax.all_to_all(jnp.stack([first_column[:width].astype(jnp.bfloat16)] * la...  14.8 us
    dot_general x1, matrix products, shards(): jnp.dot(rows_all, factor_inverse.T, precision=hi, preferred_element_type=...  14.6 us
  transfers between devices with their start and end apart: 7, of which 2 were waited for; matrix products, arithmetic and copies ran while one was open for 60% of the time, Pallas kernels for 0%

profile of v1, /device:TPU:23, one launch (start us, length us, event | category | flops | bytes accessed | tf_op | source)
XLA Modules:
  0.0 549.3 jit_solution(12780367596143964777)
XLA Ops:
  8.8 1.9 gather_fusion
  11.4 10.6 %all-to-all-start = ((s32[128,1,2]{2,1,0:T(1,128)}), s32[128,1,2]{2,1,0:T(1,128)S(1)}, u32[]{:S(2)}, u32[]{:S(2)}) async-start(s32[128,1,2]{2,1,0:T(1,128)} %bitcast.4), calls=%async_computation | async-start | bytes 131072 | tf_op jit(solution)/shard_map/all_to_all | solution.py:77
  23.1 3.6 fusion.28
  26.8 10.2 %gather_fusion.1 = bf16[256,128,128]{2,1,0:T(8,128)(2,1)} fusion(bf16[64,128,128]{2,1,0:T(8,128)(2,1)} %fusion.28, s32[1024]{0:T(1024)S(1)} %pad_clamp_fusion), kind=kCustom, calls=%fused_computation.1 | custom fusion | bytes 16778240 | tf_op jit(solution)/shard_map/jit(_take)/gather | solution.py:66
  37.0 7.4 %select_select_fusion = bf16[128,2,128,128]{3,2,1,0:T(8,128)(2,1)} fusion(bf16[128,2,128,128]{3,2,1,0:T(8,128)(2,1)} %bitcast.217, pred[128,2]{1,0:T(8,128)(4,1)S(1)} %compare_and_fusion, pred[128,2]{1,0:T(8,128)(4,1)S(1)} %broadcast_in_dim.106), kind=kLoop, calls=%fused_computation.8 | loop fusion | flops 8388608 | bytes 16777728 | tf_op jit(solution)/shard_map/jit(_where)/select_n | solution.py:64
  44.4 10.2 %all-to-all-start.1 = ((bf16[128,2,128,128]{3,2,1,0:T(8,128)(2,1)}), bf16[128,2,128,128]{3,2,1,0:T(8,128)(2,1)}, u32[]{:S(2)}, u32[]{:S(2)}) async-start(bf16[128,2,128,128]{3,2,1,0:T(8,128)(2,1)} %select_select_fusion), calls=%async_computation.1 | async-start | bytes 16777216 | tf_op jit(solution)/shard_map/all_to_all | solution.py:70
  55.2 10.7 %copy.218 = f32[1,1024,1,2048]{3,1,2,0:T(8,128)} copy(f32[1,1024,1,2048]{3,2,1,0:T(1,128)} %param.52) | data formatting | bytes 16777216
  67.3 85.8 %all-to-all-done.1 = bf16[128,2,128,128]{3,2,1,0:T(8,128)(2,1)} async-done(((bf16[128,2,128,128]{3,2,1,0:T(8,128)(2,1)}), bf16[128,2,128,128]{3,2,1,0:T(8,128)(2,1)}, u32[]{:S(2)}, u32[]{:S(2)}) %all-to-all-start.1) | async-done | bytes 8388640 | tf_op jit(solution)/shard_map/all_to_all | solution.py:70
  153.1 7.8 %fusion.139 = f32[8,16384]{1,0:T(8,128)S(1)} fusion(s32[256]{0:T(256)S(1)} %eq.128, s32[8]{0:T(128)S(1)} %iota_multiply_fusion, bf16[32,8,128,128]{3,2,1,0:T(8,128)(2,1)} %bitcast.80), kind=kOutput, calls=%fused_computation.235 | convolution fusion | flops 67110912 | bytes 8913952 | tf_op jit(solution)/shard_map/dot_general | solution.py:96
  162.3 14.8 %all_to_all.16 = bf16[8,128,128]{1,2,0:T(8,128)(2,1)S(1)} all-to-all(bf16[8,128,128]{1,2,0:T(8,128)(2,1)S(1)} %stack.75), channel_id=1, replica_groups=mesh['frow'=16,'fcol'=8] {'fcol'}, dimensions={0} | all-to-all | bytes 524288 | tf_op jit(solution)/shard_map/all_to_all | solution.py:107
  178.3 23.5 %copy.217 = bf16[32,8,128,128]{3,1,2,0:T(8,128)(2,1)} copy(bf16[32,8,128,128]{3,2,1,0:T(8,128)(2,1)} %bitcast.80) | data formatting | bytes 16777216
  201.8 11.9 %copy.142 = bf16[256,16384]{0,1:T(8,128)(2,1)} copy(bf16[256,16384]{1,0:T(8,128)(2,1)} %bitcast.218) | data formatting | bytes 16777216 | tf_op jit(solution)/shard_map/reshape | solution.py:97
  213.8 9.6 %fusion.90 = f32[8,16,128,128]{3,1,2,0:T(8,128)} fusion(bf16[128,128,256,1]{2,1,0,3:T(8,128)(2,1)} %bitcast.221, s32[8,16]{1,0:T(8,128)S(1)} %multiply_add_fusion, s32[256]{0:T(256)S(1)} %eq.128), kind=kOutput, calls=%fused_computation.114 | convolution fusion | flops 1073774592 | bytes 16778752 | tf_op jit(solution)/shard_map/dot_general | solution.py:85
  223.4 17.4 %bitcast_add_fusion = f32[1024,2048]{1,0:T(8,128)} fusion(f32[128,8,16,128]{3,2,1,0:T(8,128)} %bitcast.220, f32[1,1024,1,2048]{3,2,1,0:T(1,128)} %param.52), kind=kLoop, calls=%fused_computation.2 | loop fusion | flops 2097152 | bytes 25165824 | tf_op jit(solution)/shard_map/add | solution.py:93
  240.8 1.3 slice.718
  243.7 11.7 %cholesky.134 = f32[128,128]{1,0:T(8,128)S(1)} custom-call(f32[128,128]{1,0:T(8,128)S(1)} %copy.149), custom_call_target="Cholesky" | custom-call | tf_op jit(solution)/shard_map/jit(cholesky)/cholesky | solution.py:161
  256.8 9.8 %custom-call.12 = f32[1,128,128]{1,2,0:T(8,128)S(1)} custom-call(f32[1,128,128]{2,1,0:T(8,128)S(1)} %get-tuple-element.281), custom_call_target="InvertDiagBlocksLowerTriangular" | custom-call | tf_op jit(solution)/shard_map/triangular_solve/custom-call.0 | solution.py:162
  266.6 2.5 scatter.54
  272.8 12.1 %cholesky.145 = f32[128,128]{1,0:T(8,128)S(1)} custom-call(f32[128,128]{1,0:T(8,128)S(1)} %copy.156), custom_call_target="Cholesky" | custom-call | tf_op jit(solution)/shard_map/jit(cholesky)/cholesky | solution.py:161
  286.8 9.8 %custom-call.13 = f32[1,128,128]{1,2,0:T(8,128)S(1)} custom-call(f32[1,128,128]{2,1,0:T(8,128)S(1)} %get-tuple-element.310), custom_call_target="InvertDiagBlocksLowerTriangular" | custom-call | tf_op jit(solution)/shard_map/triangular_solve/custom-call.0 | solution.py:162
  297.5 1.5 constant_dynamic-update-slice_fusion.5
  300.3 11.7 %cholesky.156 = f32[128,128]{1,0:T(8,128)S(1)} custom-call(f32[128,128]{1,0:T(8,128)S(1)} %copy.163), custom_call_target="Cholesky" | custom-call | tf_op jit(solution)/shard_map/jit(cholesky)/cholesky | solution.py:161
  314.0 9.8 %custom-call.14 = f32[1,128,128]{1,2,0:T(8,128)S(1)} custom-call(f32[1,128,128]{2,1,0:T(8,128)S(1)} %get-tuple-element.308), custom_call_target="InvertDiagBlocksLowerTriangular" | custom-call | tf_op jit(solution)/shard_map/triangular_solve/custom-call.0 | solution.py:162
  324.7 1.4 constant_dynamic-update-slice_fusion.4
  326.9 11.7 %cholesky.167 = f32[128,128]{1,0:T(8,128)S(1)} custom-call(f32[128,128]{1,0:T(8,128)S(1)} %fusion.105), custom_call_target="Cholesky" | custom-call | tf_op jit(solution)/shard_map/jit(cholesky)/cholesky | solution.py:161
  340.6 10.0 %custom-call.15 = f32[1,128,128]{1,2,0:T(8,128)S(1)} custom-call(f32[1,128,128]{2,1,0:T(8,128)S(1)} %get-tuple-element.306), custom_call_target="InvertDiagBlocksLowerTriangular" | custom-call | tf_op jit(solution)/shard_map/triangular_solve/custom-call.0 | solution.py:162
  353.3 5.5 fusion.31
  358.8 1.3 copy-done.2
  361.3 11.7 %cholesky.178 = f32[128,128]{1,0:T(8,128)S(1)} custom-call(f32[128,128]{1,0:T(8,128)S(1)} %fusion.103), custom_call_target="Cholesky" | custom-call | tf_op jit(solution)/shard_map/jit(cholesky)/cholesky | solution.py:161
  374.7 4.7 collective-permute-start
  380.6 9.8 %custom-call.16 = f32[1,128,128]{1,2,0:T(8,128)S(1)} custom-call(f32[1,128,128]{2,1,0:T(8,128)S(1)} %get-tuple-element.304), custom_call_target="InvertDiagBlocksLowerTriangular" | custom-call | tf_op jit(solution)/shard_map/triangular_solve/custom-call.0 | solution.py:162
  390.7 3.9 collective-permute-done
  395.3 1.9 constant_dynamic-update-slice_fusion.3
  397.3 1.7 fusion.37
  399.3 11.7 %cholesky.189 = f32[128,128]{1,0:T(8,128)S(1)} custom-call(f32[128,128]{1,0:T(8,128)S(1)} %fusion.101), custom_call_target="Cholesky" | custom-call | tf_op jit(solution)/shard_map/jit(cholesky)/cholesky | solution.py:161
  412.9 9.8 %custom-call.17 = f32[1,128,128]{1,2,0:T(8,128)S(1)} custom-call(f32[1,128,128]{2,1,0:T(8,128)S(1)} %get-tuple-element.302), custom_call_target="InvertDiagBlocksLowerTriangular" | custom-call | tf_op jit(solution)/shard_map/triangular_solve/custom-call.0 | solution.py:162
  424.7 12.1 %cholesky.200 = f32[128,128]{1,0:T(8,128)S(1)} custom-call(f32[128,128]{1,0:T(8,128)S(1)} %fusion.99), custom_call_target="Cholesky" | custom-call | tf_op jit(solution)/shard_map/jit(cholesky)/cholesky | solution.py:161
  438.6 9.8 %custom-call.18 = f32[1,128,128]{1,2,0:T(8,128)S(1)} custom-call(f32[1,128,128]{2,1,0:T(8,128)S(1)} %get-tuple-element.300), custom_call_target="InvertDiagBlocksLowerTriangular" | custom-call | tf_op jit(solution)/shard_map/triangular_solve/custom-call.0 | solution.py:162
  450.2 11.7 %cholesky.211 = f32[128,128]{1,0:T(8,128)S(1)} custom-call(f32[128,128]{1,0:T(8,128)S(1)} %fusion.97), custom_call_target="Cholesky" | custom-call | tf_op jit(solution)/shard_map/jit(cholesky)/cholesky | solution.py:161
  463.8 9.8 %custom-call.19 = f32[1,128,128]{1,2,0:T(8,128)S(1)} custom-call(f32[1,128,128]{2,1,0:T(8,128)S(1)} %get-tuple-element.298), custom_call_target="InvertDiagBlocksLowerTriangular" | custom-call | tf_op jit(solution)/shard_map/triangular_solve/custom-call.0 | solution.py:162
  479.6 3.1 fusion.42
  482.7 1.8 fusion.35
  484.6 1.5 fusion.163
  486.1 2.8 copy.143
  489.6 14.6 %fusion.2 = f32[3072,1024]{1,0:T(8,128)S(1)} fusion(bf16[2048,1024]{1,0:T(8,128)(2,1)S(1)} %bitcast.223, bf16[1024,1024]{1,0:T(8,128)(2,1)S(1)} %copy-done.9, f32[1,512,512]{2,1,0:T(8,128)S(1)} %copy-done.7, f32[1,512,512]{2,1,0:T(8,128)S(1)} %copy-done.6, f32[1,512,512]{2,1,0:T(8,128)S(1)} %fusion.35), kind=kOutput, calls=%fused_computation.9 | convolution fusion | flops 19344130048 | bytes 22020096 | tf_op jit(solution)/shard_map/dot_general | solution.py:208
  504.2 4.6 copy-done.4
  509.2 18.0 %fusion.15 = f32[1024,2048]{1,0:T(8,128)S(1)} fusion(f32[1024,2048]{1,0:T(8,128)} %bitcast_add_fusion, f32[3072,1024]{1,0:T(8,128)} %copy-done.4), kind=kOutput, calls=%fused_computation.27 | convolution fusion | flops 12886999040 | bytes 29360128 | tf_op jit(solution)/shard_map/dot_general | solution.py:36
  530.0 12.5 %copy.186 = f32[1,1024,1,2048]{3,2,1,0:T(1,128)} copy(f32[1,1024,1,2048]{3,1,2,0:T(8,128)S(1)} %select_bitcast_fusion) | data formatting | bytes 16777216 | tf_op jit(solution)/shard_map/broadcast_in_dim | solution.py:221
  (168 shorter events, 51.7 us)
Async XLA Ops:
  6.5 16.6 %copy-start = (bf16[64,128,128]{2,1,0:T(8,128)(2,1)S(1)}, bf16[64,128,128]{2,1,0:T(8,128)(2,1)}, u32[]{:S(2)}) copy-start(bf16[64,128,128]{2,1,0:T(8,128)(2,1)} %param.53) | copy-start | bytes 6291460
  11.4 33.0 %all-to-all-start = ((s32[128,1,2]{2,1,0:T(1,128)}), s32[128,1,2]{2,1,0:T(1,128)S(1)}, u32[]{:S(2)}, u32[]{:S(2)}) async-start(s32[128,1,2]{2,1,0:T(1,128)} %bitcast.4), calls=%async_computation | async-start | bytes 131072 | tf_op jit(solution)/shard_map/all_to_all | solution.py:77
  44.4 108.7 %all-to-all-start.1 = ((bf16[128,2,128,128]{3,2,1,0:T(8,128)(2,1)}), bf16[128,2,128,128]{3,2,1,0:T(8,128)(2,1)}, u32[]{:S(2)}, u32[]{:S(2)}) async-start(bf16[128,2,128,128]{3,2,1,0:T(8,128)(2,1)} %select_select_fusion), calls=%async_computation.1 | async-start | bytes 16777216 | tf_op jit(solution)/shard_map/all_to_all | solution.py:70
  54.6 186.1 %all-gather.6.cloned.1.call-start = ((), (), s32[]{:S(2)}) async-start(), calls=%async_computation.3 | async-start | bytes 2228224 | tf_op jit(solution)/shard_map/all_gather | solution.py:116
  162.1 39.7 %copy-start.5 = (bf16[1024,128]{1,0:T(8,128)(2,1)}, bf16[1024,128]{1,0:T(8,128)(2,1)S(1)}, u32[]{:S(2)}) copy-start(bf16[1024,128]{1,0:T(8,128)(2,1)S(1)} %slice_add_fusion) | copy-start | bytes 786436
  177.8 122.3 %all-gather.8.cloned.1.call-start = ((), (), s32[]{:S(2)}) async-start(), calls=%async_computation.4 | async-start | bytes 2228224 | tf_op jit(solution)/shard_map/all_gather | solution.py:118
  242.1 131.6 %all-gather.10.cloned.1.call-start = ((), (), s32[]{:S(2)}) async-start(), calls=%async_computation.5 | async-start | bytes 2359296 | tf_op jit(solution)/shard_map/all_gather | solution.py:121
  300.1 52.6 %slice-start = ((bf16[2048,512]{0,1:T(8,128)(2,1)}), bf16[1024,512]{0,1:T(8,128)(2,1)S(1)}, s32[]{:S(2)}) async-start(bf16[2048,512]{0,1:T(8,128)(2,1)} %all-gather.8.cloned.1.call-done), calls=%async_computation.7 | async-start | bytes 2097152 | tf_op jit(solution)/shard_map/slice | solution.py:118
  300.2 185.9 %all-gather.12.cloned.1.call-start = ((), (), s32[]{:S(2)}) async-start(), calls=%async_computation.6 | async-start | bytes 4456448 | tf_op jit(solution)/shard_map/all_gather | solution.py:133
  353.3 37.1 %copy-start.3 = (f32[8,128,128]{2,1,0:T(8,128)S(1)}, f32[8,128,128]{2,1,0:T(8,128)}, u32[]{:S(2)}) copy-start(f32[8,128,128]{2,1,0:T(8,128)} %get-tuple-element.327) | copy-start | bytes 1572868
  358.8 1.3 copy-start.2
  374.7 19.9 %collective-permute-start = (bf16[128,1024]{1,0:T(8,128)(2,1)S(1)}, bf16[128,1024]{1,0:T(8,128)(2,1)S(1)}, u32[]{:S(2)}, u32[]{:S(2)}) collective-permute-start(bf16[128,1024]{1,0:T(8,128)(2,1)S(1)} %constant_dynamic-slice_fusion), channel_id=1, source_target_pairs={{0,0},{1,8},{2,16},{3,24},{4,32},{5,40},{6,48},{7,56},{8,1},{9,9},... | collective-permute-start | bytes 786440 | tf_op jit(solution)/shard_map/ppermute | solution.py:132
  394.6 0.7 copy-start.8
  486.1 2.8 copy-start.6
  486.1 2.9 copy-start.7
  486.1 3.5 copy-start.9
  504.2 4.6 copy-start.4
  530.0 12.5 %copy-start.1 = (bf16[64,128,128]{2,1,0:T(8,128)(2,1)S(1)}, bf16[64,128,128]{2,1,0:T(8,128)(2,1)}, u32[]{:S(2)}) copy-start(bf16[64,128,128]{2,1,0:T(8,128)(2,1)} %param.53) | copy-start | bytes 6291460
Sparse Core Ops, SparseCore 0:
  177.9 46.6 all-gather.5
  242.2 47.1 all-gather.7
  300.3 28.9 all-gather.9
  395.5 51.5 all-gather.11
